TPU v7x, 512 devices: a whole 4x4x16 slice. The times are simulated.
512 devices in a mesh: head: 8 (over x, core), expert: 64 (over z, y).
Axes of the slice: x: 4, y: 4, z: 16, core: 2. Of those that a mesh axis runs over, the one named last changes fastest.
Arguments:
- q_latent: bfloat16 [512, 64, 512], P('expert', 'head'), may hold values from -16 to 16
- q_rotary: bfloat16 [512, 64, 64], P('expert', 'head'), may hold values from -3 to 3
- cache_latent: bfloat16 [512, 128, 512], P('expert'), may hold values from -5 to 5
- cache_rotary: bfloat16 [512, 64, 128], P('expert'), may hold values from -5 to 5
- lengths: int32 [512], P('expert'), may hold values from 16 to 128, as said below
- w_value_out: bfloat16 [32768, 5120], P('head', 'expert'), may hold values from -0.25 to 0.25
- resid: bfloat16 [512, 5120], P('expert'), may hold values from -8 to 8
- norm_gain: float32 [5120], replicated, may hold values from 0.1 to 1.9
- route_ids: int32 [512, 6], P('expert'), may hold values from 0 to 63, as said below
- route_weights: float32 [512, 6], P('expert'), may hold values from 0.1 to 0.6
- w_gate_up: bfloat16 [64, 2, 768, 5120], P('expert', None, 'head'), may hold values from -0.078125 to 0.078125
- w_down: bfloat16 [64, 768, 5120], P('expert', 'head'), may hold values from -0.21875 to 0.21875
Outputs:
- mixed_out: float32 [512, 5120], P('expert', 'head')
Inputs may be any that keep to these rules, and one draw needn't show every extreme that they name: `lengths`: slots at positions below a sequence's length are valid; some sequence has length 128. `route_ids`: each row names 6 different experts. Among the rows of one device (aligned blocks of 8 rows) no expert is named by more than 2 rows, and one expert is named by exactly 2 rows in every block.
All inputs are finite; a program needn't handle non-finite values.
Results may differ from a plain program's by a relative error of at most 0.0046.
Values may be sent and summed in bfloat16 or wider, within the bound.
No kernel may reach another device: no remote copies, remote signals or barrier semaphores. Data moves between devices by JAX's collectives and lax.ppermute only.
A program may use at most 64 MiB of HBM per device.

v0:
```python
import jax
import jax.numpy as jnp
from jax import lax
from jax.sharding import Mesh
from jax.sharding import PartitionSpec as P

EXPERT = ("ez", "ey")
softmax_scale = 192.0 ** (-0.5)
norm_epsilon = 1e-06


def attend(q_latent, q_rotary, cache_latent, cache_rotary, lengths):
    scores = jnp.einsum("shl,scl->shc", q_latent, cache_latent, preferred_element_type=jnp.float32)
    scores = scores + jnp.einsum(
        "shr,src->shc", q_rotary, cache_rotary, preferred_element_type=jnp.float32
    )
    scores = scores * softmax_scale
    position = lax.broadcasted_iota(jnp.int32, scores.shape, 2)
    scores = jnp.where(position < lengths[:, None, None], scores, -1e30)
    highest = jnp.max(scores, axis=2, keepdims=True)
    weights = jnp.exp(scores - highest)
    probs = (weights / jnp.sum(weights, axis=2, keepdims=True)).astype(jnp.bfloat16)
    return jnp.einsum(
        "shc,scl->shl", probs, cache_latent, preferred_element_type=jnp.float32
    ).astype(jnp.bfloat16)


def on_device(
    q_latent,
    q_rotary,
    cache_latent,
    cache_rotary,
    lengths,
    w_value_out,
    resid,
    norm_gain,
    route_ids,
    route_weights,
    w_gate_up,
    w_down,
):
    seq_local = q_latent.shape[0]
    latent_out = attend(q_latent, q_rotary, cache_latent, cache_rotary, lengths)
    flattened = latent_out.reshape(seq_local, -1)
    z_count = lax.axis_size("ez")
    latent_copies = jnp.broadcast_to(flattened[None], (z_count,) + flattened.shape)
    gathered = lax.all_to_all(latent_copies, "ez", split_axis=0, concat_axis=0, tiled=True)
    gathered = gathered.reshape(-1, flattened.shape[1])
    value_blocks = lax.all_gather(w_value_out, "ey", axis=0, tiled=False)
    column_terms = jnp.einsum(
        "sk,jkc->sjc", gathered, value_blocks, preferred_element_type=jnp.float32
    ).reshape(gathered.shape[0], -1)
    column_sums = lax.psum(column_terms, "head")
    attention = lax.all_to_all(
        column_sums.astype(jnp.bfloat16), "ez", split_axis=0, concat_axis=1, tiled=True
    )
    stream = resid.astype(jnp.float32) + attention.astype(jnp.float32)
    mean_square = jnp.mean(stream * stream, axis=1, keepdims=True)
    normed = (stream * lax.rsqrt(mean_square + norm_epsilon) * norm_gain).astype(jnp.bfloat16)
    expert_count = lax.axis_size("ez") * lax.axis_size("ey")
    top_count = route_ids.shape[1]
    capacity = max(2, -(-(seq_local * top_count) // expert_count))
    flat_ids = route_ids.reshape(-1)
    one_hot = (flat_ids[:, None] == jnp.arange(expert_count, dtype=jnp.int32)[None, :]).astype(
        jnp.int32
    )
    earlier = jnp.cumsum(one_hot, axis=0) - one_hot
    slot_index = jnp.sum(earlier * one_hot, axis=1)
    target = (flat_ids * capacity + slot_index).reshape(seq_local, top_count)
    places = jnp.arange(expert_count * capacity, dtype=jnp.int32)
    matches = target[None, :, :] == places[:, None, None]
    selector = jnp.sum(matches.astype(jnp.int32), axis=2).astype(jnp.bfloat16)
    blending = jnp.sum(jnp.where(matches, route_weights[None, :, :], 0.0), axis=2)
    gate_up = w_gate_up[0]
    col_width = stream.shape[1] // lax.axis_size("head")
    offset = lax.axis_index("head") * col_width
    normed_cols = lax.dynamic_slice_in_dim(normed, offset, col_width, 1)
    outgoing = jnp.dot(selector, normed_cols, preferred_element_type=jnp.float32).astype(
        jnp.bfloat16
    )
    outgoing = outgoing.reshape(expert_count, capacity, -1)
    arrived = lax.all_to_all(outgoing, EXPERT, split_axis=0, concat_axis=0, tiled=True)
    arrived_cols = arrived.reshape(-1, arrived.shape[2])
    head_count = lax.axis_size("head")
    down_blocks = w_down[0].reshape(w_down.shape[1], head_count, -1)
    arrived_cols, down_blocks = lax.optimization_barrier((arrived_cols, down_blocks))
    down_cols = lax.all_to_all(down_blocks, "head", split_axis=1, concat_axis=0, tiled=True)
    down_cols = down_cols.reshape(-1, down_blocks.shape[2])
    flat_rows = lax.all_gather(arrived_cols, "head", axis=1, tiled=True)
    projected = jnp.einsum("rd,gfd->rgf", flat_rows, gate_up, preferred_element_type=jnp.float32)
    hidden = (jax.nn.silu(projected[:, 0]) * projected[:, 1]).astype(jnp.bfloat16)
    hidden_all = lax.all_gather(hidden, "head", axis=1, tiled=True)
    summed_cols = jnp.dot(hidden_all, down_cols, preferred_element_type=jnp.float32).astype(
        jnp.bfloat16
    )
    summed_rows = summed_cols.reshape(expert_count, capacity, -1)
    returned = lax.all_to_all(summed_rows, EXPERT, split_axis=0, concat_axis=0, tiled=True)
    back_rows = returned.reshape(expert_count * capacity, -1).astype(jnp.float32)
    mixture = jnp.dot(blending.T, back_rows, precision=lax.Precision.HIGHEST)
    stream_cols = lax.dynamic_slice_in_dim(stream, offset, col_width, 1)
    return stream_cols + mixture


def solution(mesh):
    placed = (
        P(EXPERT, "head", None),
        P(EXPERT, "head", None),
        P(EXPERT, None, None),
        P(EXPERT, None, None),
        P(EXPERT),
        P("head", EXPERT),
        P(EXPERT, None),
        P(),
        P(EXPERT, None),
        P(EXPERT, None),
        P(EXPERT, None, "head", None),
        P(EXPERT, "head", None),
    )
    head_count, expert_total = mesh.devices.shape
    y_count = len({device.coords[1] for device in mesh.devices[0]})
    split_mesh = Mesh(
        mesh.devices.reshape(head_count, expert_total // y_count, y_count), ("head",) + EXPERT
    )
    return jax.shard_map(
        on_device, mesh=split_mesh, in_specs=placed, out_specs=P(EXPERT, "head"), check_vma=False
    )
```

profile of v0, /device:TPU:8, one launch (start us, length us, event | category | flops | bytes accessed | tf_op | source)
XLA Modules:
  0.0 234.2 jit_solution(10736050746131402408)
XLA Ops:
  7.3 1.6 fusion.20
  8.9 1.1 fusion.8
  10.5 1.1 broadcast_in_dim.33
  11.6 15.2 %all-to-all-start = ((bf16[16,8,4096]{2,1,0:T(8,128)(2,1)}), bf16[16,8,4096]{2,1,0:T(8,128)(2,1)S(1)}, u32[]{:S(2)}, u32[]{:S(2)}) async-start(bf16[16,8,4096]{2,1,0:T(8,128)(2,1)} %broadcast_in_dim.33), calls=%async_computation | async-start | bytes 2097152 | tf_op jit(solution)/shard_map/all_to_all | solution.py:47
  27.3 28.6 %all-gather.6.cloned.1.call-done = bf16[16384,80]{0,1:T(8,128)(2,1)} async-done(((bf16[4096,80]{0,1:T(8,128)(2,1)}), bf16[16384,80]{0,1:T(8,128)(2,1)}) %all-gather.6.cloned.1.call-update) | async-done | bytes 2621456 | tf_op jit(solution)/shard_map/all_gather | solution.py:49
  55.9 5.5 %reshape.55 = bf16[4,4096,80]{1,0,2:T(4,128)(2,1)} reshape(bf16[16384,80]{0,1:T(8,128)(2,1)} %all-gather.6.cloned.1.call-done) | data formatting | bytes 5242880 | tf_op jit(solution)/shard_map/all_gather | solution.py:49
  61.4 4.7 %copy.24 = bf16[4,80,4096]{2,1,0:T(8,128)(2,1)} copy(bf16[4,80,4096]{2,0,1:T(4,128)(2,1)} %bitcast.50) | data formatting | bytes 5242880 | tf_op jit(solution)/shard_map/sk,jkc->sjc/dot_general | solution.py:50
  66.1 10.7 %all-to-all-done = bf16[16,8,4096]{2,1,0:T(8,128)(2,1)S(1)} async-done(((bf16[16,8,4096]{2,1,0:T(8,128)(2,1)}), bf16[16,8,4096]{2,1,0:T(8,128)(2,1)S(1)}, u32[]{:S(2)}, u32[]{:S(2)}) %all-to-all-start) | async-done | bytes 1048608 | tf_op jit(solution)/shard_map/all_to_all | solution.py:47
  76.8 2.6 %fusion.9 = f32[128,320]{0,1:T(8,128)S(1)} fusion(bf16[320,4096]{1,0:T(8,128)(2,1)} %bitcast.49, bf16[16,8,4096]{2,1,0:T(8,128)(2,1)S(1)} %all-to-all-done), kind=kOutput, calls=%fused_computation.14 | convolution fusion | flops 335544320 | bytes 3833856 | tf_op jit(solution)/shard_map/sk,jkc->sjc/dot_general | solution.py:50
  79.4 25.1 %all-reduce.1 = bf16[128,320]{0,1:T(8,128)(2,1)S(1)} all-reduce(f32[128,320]{0,1:T(8,128)S(1)} %fusion.9), channel_id=1, replica_groups=mesh['head'=8,'ez'=16,'ey'=4] {'head'}, use_global_device_ids=true, to_apply=%region_2.3 | all-reduce | flops 40960 | bytes 245760 | tf_op jit(solution)/shard_map/psum | solution.py:53
  105.2 10.2 %all-to-all-start.1 = ((bf16[16,8,320]{2,1,0:T(8,128)(2,1)}), bf16[16,8,320]{2,1,0:T(8,128)(2,1)S(1)}, u32[]{:S(2)}, u32[]{:S(2)}) async-start(bf16[16,8,320]{2,1,0:T(8,128)(2,1)} %bitcast.3), calls=%async_computation.1 | async-start | bytes 196608 | tf_op jit(solution)/shard_map/all_to_all | solution.py:54
  115.6 0.8 dynamic-slice
  116.4 12.1 %all-to-all-done.1 = bf16[16,8,320]{2,1,0:T(8,128)(2,1)S(1)} async-done(((bf16[16,8,320]{2,1,0:T(8,128)(2,1)}), bf16[16,8,320]{2,1,0:T(8,128)(2,1)S(1)}, u32[]{:S(2)}, u32[]{:S(2)}) %all-to-all-start.1) | async-done | bytes 81952 | tf_op jit(solution)/shard_map/all_to_all | solution.py:54
  129.9 7.0 %all-to-all-start.2 = ((bf16[64,2,640]{2,1,0:T(2,128)(2,1)}), bf16[64,2,640]{2,1,0:T(2,128)(2,1)S(1)}, u32[]{:S(2)}, u32[]{:S(2)}) async-start(bf16[64,2,640]{2,1,0:T(2,128)(2,1)} %reshape.49), calls=%async_computation.2 | async-start | bytes 327680 | tf_op jit(solution)/shard_map/all_to_all | solution.py:82
  136.9 1.3 copy.31
  138.2 14.4 %all-to-all-done.2 = bf16[64,2,640]{2,1,0:T(2,128)(2,1)S(1)} async-done(((bf16[64,2,640]{2,1,0:T(2,128)(2,1)}), bf16[64,2,640]{2,1,0:T(2,128)(2,1)S(1)}, u32[]{:S(2)}, u32[]{:S(2)}) %all-to-all-start.2) | async-done | bytes 163872 | tf_op jit(solution)/shard_map/all_to_all | solution.py:82
  153.3 1.1 copy.29
  154.4 5.0 %all-to-all-start.3 = ((bf16[96,8,640]{2,0,1:T(8,128)(2,1)}), bf16[96,8,640]{2,0,1:T(8,128)(2,1)S(1)}, u32[]{:S(2)}, u32[]{:S(2)}) async-start(bf16[96,8,640]{2,0,1:T(8,128)(2,1)} %copy.29), calls=%async_computation.3 | async-start | bytes 1966080 | tf_op jit(solution)/shard_map/all_to_all | solution.py:87
  159.4 19.3 %all-gather.4.cloned.1.call-done = bf16[128,5120]{1,0:T(8,128)(2,1)} async-done(((bf16[128,640]{1,0:T(8,128)(2,1)}), bf16[128,5120]{1,0:T(8,128)(2,1)}) %all-gather.4.cloned.1.call-update) | async-done | bytes 1310736 | tf_op jit(solution)/shard_map/all_gather | solution.py:89
  178.7 2.0 fusion.1
  180.8 12.8 %all_gather.15 = bf16[128,768]{0,1:T(8,128)(2,1)S(1)} all-gather(bf16[128,96]{0,1:T(8,128)(2,1)S(1)} %fusion.12), channel_id=1, replica_groups=mesh['head'=8,'ez'=16,'ey'=4] {'head'}, dimensions={1}, use_global_device_ids=true | all-gather | bytes 221184 | tf_op jit(solution)/shard_map/all_gather | solution.py:92
  194.6 13.5 %all-to-all-start.4 = ((bf16[64,2,640]{2,1,0:T(2,128)(2,1)}), bf16[64,2,640]{2,1,0:T(2,128)(2,1)S(1)}, u32[]{:S(2)}, u32[]{:S(2)}) async-start(bf16[64,2,640]{2,1,0:T(2,128)(2,1)} %reshape.52), calls=%async_computation.4 | async-start | bytes 327680 | tf_op jit(solution)/shard_map/all_to_all | solution.py:97
  208.3 18.2 %all-to-all-done.4 = bf16[64,2,640]{2,1,0:T(2,128)(2,1)S(1)} async-done(((bf16[64,2,640]{2,1,0:T(2,128)(2,1)}), bf16[64,2,640]{2,1,0:T(2,128)(2,1)S(1)}, u32[]{:S(2)}, u32[]{:S(2)}) %all-to-all-start.4) | async-done | bytes 163872 | tf_op jit(solution)/shard_map/all_to_all | solution.py:97
  226.6 0.8 convolution_add_fusion.1
  (41 shorter events, 6.1 us)
Async XLA Ops:
  6.5 172.2 %copy-start = (bf16[1,2,96,5120]{3,2,1,0:T(8,128)(2,1)S(1)}, bf16[1,2,96,5120]{3,2,1,0:T(8,128)(2,1)}, u32[]{:S(2)}) copy-start(bf16[1,2,96,5120]{3,2,1,0:T(8,128)(2,1)} %param.22) | copy-start | bytes 5898244
  6.5 3.6 %copy-start.1 = (bf16[8,128,512]{2,1,0:T(8,128)(2,1)S(1)}, bf16[8,128,512]{2,1,0:T(8,128)(2,1)}, u32[]{:S(2)}) copy-start(bf16[8,128,512]{2,1,0:T(8,128)(2,1)} %param.14) | copy-start | bytes 3145732
  6.5 49.3 %all-gather.6.cloned.1.call-start = ((), (), s32[]{:S(2)}) async-start(), calls=%async_computation.6 | async-start | bytes 3276800 | tf_op jit(solution)/shard_map/all_gather | solution.py:49
  10.4 16.4 %copy-start.3 = (s32[8,6]{1,0:T(8,128)S(1)}, s32[8,6]{1,0:T(8,128)}, u32[]{:S(2)}) copy-start(s32[8,6]{1,0:T(8,128)} %param.20) | copy-start | bytes 580
  11.6 65.2 %all-to-all-start = ((bf16[16,8,4096]{2,1,0:T(8,128)(2,1)}), bf16[16,8,4096]{2,1,0:T(8,128)(2,1)S(1)}, u32[]{:S(2)}, u32[]{:S(2)}) async-start(bf16[16,8,4096]{2,1,0:T(8,128)(2,1)} %broadcast_in_dim.33), calls=%async_computation | async-start | bytes 2097152 | tf_op jit(solution)/shard_map/all_to_all | solution.py:47
  76.8 51.9 %copy-start.2 = (bf16[8,5120]{1,0:T(8,128)(2,1)S(1)}, bf16[8,5120]{1,0:T(8,128)(2,1)}, u32[]{:S(2)}) copy-start(bf16[8,5120]{1,0:T(8,128)(2,1)} %param.18) | copy-start | bytes 245764
  105.2 23.2 %all-to-all-start.1 = ((bf16[16,8,320]{2,1,0:T(8,128)(2,1)}), bf16[16,8,320]{2,1,0:T(8,128)(2,1)S(1)}, u32[]{:S(2)}, u32[]{:S(2)}) async-start(bf16[16,8,320]{2,1,0:T(8,128)(2,1)} %bitcast.3), calls=%async_computation.1 | async-start | bytes 196608 | tf_op jit(solution)/shard_map/all_to_all | solution.py:54
  129.9 22.7 %all-to-all-start.2 = ((bf16[64,2,640]{2,1,0:T(2,128)(2,1)}), bf16[64,2,640]{2,1,0:T(2,128)(2,1)S(1)}, u32[]{:S(2)}, u32[]{:S(2)}) async-start(bf16[64,2,640]{2,1,0:T(2,128)(2,1)} %reshape.49), calls=%async_computation.2 | async-start | bytes 327680 | tf_op jit(solution)/shard_map/all_to_all | solution.py:82
  136.8 41.9 %all-gather.4.cloned.1.call-start = ((), (), s32[]{:S(2)}) async-start(), calls=%async_computation.5 | async-start | bytes 1474560 | tf_op jit(solution)/shard_map/all_gather | solution.py:89
  154.4 39.1 %all-to-all-start.3 = ((bf16[96,8,640]{2,0,1:T(8,128)(2,1)}), bf16[96,8,640]{2,0,1:T(8,128)(2,1)S(1)}, u32[]{:S(2)}, u32[]{:S(2)}) async-start(bf16[96,8,640]{2,0,1:T(8,128)(2,1)} %copy.29), calls=%async_computation.3 | async-start | bytes 1966080 | tf_op jit(solution)/shard_map/all_to_all | solution.py:87
  180.7 27.4 %copy-start.4 = (f32[8,6]{1,0:T(8,128)S(1)}, f32[8,6]{1,0:T(8,128)}, u32[]{:S(2)}) copy-start(f32[8,6]{1,0:T(8,128)} %param.21) | copy-start | bytes 580
  194.6 31.9 %all-to-all-start.4 = ((bf16[64,2,640]{2,1,0:T(2,128)(2,1)}), bf16[64,2,640]{2,1,0:T(2,128)(2,1)S(1)}, u32[]{:S(2)}, u32[]{:S(2)}) async-start(bf16[64,2,640]{2,1,0:T(2,128)(2,1)} %reshape.52), calls=%async_computation.4 | async-start | bytes 327680 | tf_op jit(solution)/shard_map/all_to_all | solution.py:97
Sparse Core Ops, SparseCore 0:
  9.5 46.3 all-gather.5
  153.5 25.2 all-gather.3
where the time goes:
time: 235 us; the launch traced here: 234 us
  waiting for transfers between devices  104 us (44%)
  starting transfers between devices  50.9 us (22%)
  blocking collectives  37.9 us (16%)
  local copies, waits for them, and re-layouts  18 us (8%)
  between operations  13.6 us (6%)
  matrix products  9.05 us (4%)
    all_gather x1, waiting for transfers between devices, on_device(): value_blocks = lax.all_gather(w_value_out, 'ey', axis=0, tiled=False)  28.6 us
    psum x1, blocking collectives, on_device(): column_sums = lax.psum(column_terms, 'head')  25.1 us
    all_gather x1, waiting for transfers between devices, on_device(): flat_rows = lax.all_gather(arrived_cols, 'head', axis=1, tiled=True)  19.3 us
    all_to_all x1, waiting for transfers between devices, on_device(): lax.all_to_all(summed_rows, EXPERT, split_axis=0, concat_axis=0, tiled=True)  18.2 us
    all_to_all x1, starting transfers between devices, on_device(): lax.all_to_all(latent_copies, 'ez', split_axis=0, concat_axis=0, tiled=True)  15.2 us
    all_to_all x1, waiting for transfers between devices, on_device(): lax.all_to_all(outgoing, EXPERT, split_axis=0, concat_axis=0, tiled=True)  14.4 us
    all_to_all x1, starting transfers between devices, on_device(): lax.all_to_all(summed_rows, EXPERT, split_axis=0, concat_axis=0, tiled=True)  13.5 us
    all_gather x1, blocking collectives, on_device(): hidden_all = lax.all_gather(hidden, 'head', axis=1, tiled=True)  12.8 us
  transfers between devices with their start and end apart: 7, of which 6 were waited for; matrix products, arithmetic and copies ran while one was open for 9% of the time, Pallas kernels for 0%

commit v1 on v0

--- a/solution.py
+++ b/solution.py
@@ -50,7 +50,7 @@
     column_terms = jnp.einsum(
         "sk,jkc->sjc", gathered, value_blocks, preferred_element_type=jnp.float32
     ).reshape(gathered.shape[0], -1)
-    column_sums = lax.psum(column_terms, "head")
+    column_sums = jnp.sum(lax.all_gather(column_terms, "head"), axis=0)
     attention = lax.all_to_all(
         column_sums.astype(jnp.bfloat16), "ez", split_axis=0, concat_axis=1, tiled=True
     )

time: 235 us -> 246 us (1.047)
  waiting for transfers between devices: 104 us -> 136 us
  blocking collectives: 37.9 us -> 12.8 us
    all_gather x0 -> x1, waiting for transfers between devices: none -> 28.6 us  [on_device(): column_sums = jnp.sum(lax.all_gather(column_terms, 'head'), axis=0)]
    psum x1 -> x0, blocking collectives: 25.1 us -> none  [on_device(): column_sums = lax.psum(column_terms, 'head')]
  transfers between devices with their start and end apart: 7 -> 8, of which waited for: 6 -> 7; matrix products, arithmetic and copies ran while one was open for 9% -> 8% of each run, Pallas kernels for 0% -> 0%
where the time goes in v1:
time: 246 us; the launch traced here: 245 us
  waiting for transfers between devices  136 us (55%)
  starting transfers between devices  52.2 us (21%)
  local copies, waits for them, and re-layouts  19.6 us (8%)
  between operations  13.3 us (5%)
  blocking collectives  12.8 us (5%)
  matrix products  9.69 us (4%)
    all_gather x1, waiting for transfers between devices, on_device(): value_blocks = lax.all_gather(w_value_out, 'ey', axis=0, tiled=False)  29 us
    all_gather x1, waiting for transfers between devices, on_device(): column_sums = jnp.sum(lax.all_gather(column_terms, 'head'), axis=0)  28.6 us
    all_gather x1, waiting for transfers between devices, on_device(): flat_rows = lax.all_gather(arrived_cols, 'head', axis=1, tiled=True)  19.3 us
    all_to_all x1, waiting for transfers between devices, on_device(): lax.all_to_all(summed_rows, EXPERT, split_axis=0, concat_axis=0, tiled=True)  18.2 us
    all_to_all x1, waiting for transfers between devices, on_device(): lax.all_to_all(outgoing, EXPERT, split_axis=0, concat_axis=0, tiled=True)  16.4 us
    all_to_all x1, starting transfers between devices, on_device(): lax.all_to_all(latent_copies, 'ez', split_axis=0, concat_axis=0, tiled=True)  15.2 us
    all_to_all x1, starting transfers between devices, on_device(): lax.all_to_all(summed_rows, EXPERT, split_axis=0, concat_axis=0, tiled=True)  13.5 us
    all_to_all x1, waiting for transfers between devices, on_device(): lax.all_to_all(column_sums.astype(jnp.bfloat16), 'ez', split_axis=0, conc...  12.9 us
  transfers between devices with their start and end apart: 8, of which 7 were waited for; matrix products, arithmetic and copies ran while one was open for 8% of the time, Pallas kernels for 0%

profile of v1, /device:TPU:8, one launch (start us, length us, event | category | flops | bytes accessed | tf_op | source)
XLA Modules:
  0.0 244.7 jit_solution(15456704418381969590)
XLA Ops:
  7.3 1.6 fusion.20
  8.9 1.1 fusion.8
  10.5 1.1 broadcast_in_dim.33
  11.6 15.2 %all-to-all-start = ((bf16[16,8,4096]{2,1,0:T(8,128)(2,1)}), bf16[16,8,4096]{2,1,0:T(8,128)(2,1)S(1)}, u32[]{:S(2)}, u32[]{:S(2)}) async-start(bf16[16,8,4096]{2,1,0:T(8,128)(2,1)} %broadcast_in_dim.33), calls=%async_computation | async-start | bytes 2097152 | tf_op jit(solution)/shard_map/all_to_all | solution.py:47
  26.9 29.0 %all-gather.8.cloned.1.call-done = bf16[16384,80]{0,1:T(8,128)(2,1)} async-done(((bf16[4096,80]{0,1:T(8,128)(2,1)}), bf16[16384,80]{0,1:T(8,128)(2,1)}) %all-gather.8.cloned.1.call-update) | async-done | bytes 2621456 | tf_op jit(solution)/shard_map/all_gather | solution.py:49
  55.9 5.5 %reshape.61 = bf16[4,4096,80]{1,0,2:T(4,128)(2,1)} reshape(bf16[16384,80]{0,1:T(8,128)(2,1)} %all-gather.8.cloned.1.call-done) | data formatting | bytes 5242880 | tf_op jit(solution)/shard_map/all_gather | solution.py:49
  61.4 4.7 %copy.21 = bf16[4,80,4096]{2,1,0:T(8,128)(2,1)} copy(bf16[4,80,4096]{2,0,1:T(4,128)(2,1)} %bitcast.55) | data formatting | bytes 5242880 | tf_op jit(solution)/shard_map/sk,jkc->sjc/dot_general | solution.py:50
  66.1 10.7 %all-to-all-done = bf16[16,8,4096]{2,1,0:T(8,128)(2,1)S(1)} async-done(((bf16[16,8,4096]{2,1,0:T(8,128)(2,1)}), bf16[16,8,4096]{2,1,0:T(8,128)(2,1)S(1)}, u32[]{:S(2)}, u32[]{:S(2)}) %all-to-all-start) | async-done | bytes 1048608 | tf_op jit(solution)/shard_map/all_to_all | solution.py:47
  76.8 3.2 %fusion.9 = f32[128,320]{0,1:T(8,128)} fusion(bf16[320,4096]{1,0:T(8,128)(2,1)} %bitcast.54, bf16[16,8,4096]{2,1,0:T(8,128)(2,1)S(1)} %all-to-all-done), kind=kOutput, calls=%fused_computation.15 | convolution fusion | flops 335544320 | bytes 3833856 | tf_op jit(solution)/shard_map/sk,jkc->sjc/dot_general | solution.py:50
  80.6 28.6 %all-gather.10.cloned.1.call-done = f32[1024,320]{0,1:T(8,128)} async-done(((f32[128,320]{0,1:T(8,128)}), f32[1024,320]{0,1:T(8,128)}) %all-gather.10.cloned.1.call-update) | async-done | bytes 1310736 | tf_op jit(solution)/shard_map/all_gather | solution.py:53
  109.2 1.6 copy.28
  111.8 12.3 %all-to-all-start.1 = ((bf16[16,8,320]{2,1,0:T(8,128)(2,1)}), bf16[16,8,320]{2,1,0:T(8,128)(2,1)S(1)}, u32[]{:S(2)}, u32[]{:S(2)}) async-start(bf16[16,8,320]{2,1,0:T(8,128)(2,1)} %bitcast.3), calls=%async_computation.1 | async-start | bytes 196608 | tf_op jit(solution)/shard_map/all_to_all | solution.py:54
  125.1 12.9 %all-to-all-done.1 = bf16[16,8,320]{2,1,0:T(8,128)(2,1)S(1)} async-done(((bf16[16,8,320]{2,1,0:T(8,128)(2,1)}), bf16[16,8,320]{2,1,0:T(8,128)(2,1)S(1)}, u32[]{:S(2)}, u32[]{:S(2)}) %all-to-all-start.1) | async-done | bytes 81952 | tf_op jit(solution)/shard_map/all_to_all | solution.py:54
  139.3 7.2 %all-to-all-start.2 = ((bf16[64,2,640]{2,1,0:T(2,128)(2,1)}), bf16[64,2,640]{2,1,0:T(2,128)(2,1)S(1)}, u32[]{:S(2)}, u32[]{:S(2)}) async-start(bf16[64,2,640]{2,1,0:T(2,128)(2,1)} %reshape.55), calls=%async_computation.2 | async-start | bytes 327680 | tf_op jit(solution)/shard_map/all_to_all | solution.py:82
  146.6 1.3 copy.29
  147.9 16.4 %all-to-all-done.2 = bf16[64,2,640]{2,1,0:T(2,128)(2,1)S(1)} async-done(((bf16[64,2,640]{2,1,0:T(2,128)(2,1)}), bf16[64,2,640]{2,1,0:T(2,128)(2,1)S(1)}, u32[]{:S(2)}, u32[]{:S(2)}) %all-to-all-start.2) | async-done | bytes 163872 | tf_op jit(solution)/shard_map/all_to_all | solution.py:82
  165.0 1.1 copy.26
  166.1 4.0 %all-to-all-start.3 = ((bf16[96,8,640]{2,0,1:T(8,128)(2,1)}), bf16[96,8,640]{2,0,1:T(8,128)(2,1)S(1)}, u32[]{:S(2)}, u32[]{:S(2)}) async-start(bf16[96,8,640]{2,0,1:T(8,128)(2,1)} %copy.26), calls=%async_computation.3 | async-start | bytes 1966080 | tf_op jit(solution)/shard_map/all_to_all | solution.py:87
  170.1 19.3 %all-gather.6.cloned.1.call-done = bf16[128,5120]{1,0:T(8,128)(2,1)} async-done(((bf16[128,640]{1,0:T(8,128)(2,1)}), bf16[128,5120]{1,0:T(8,128)(2,1)}) %all-gather.6.cloned.1.call-update) | async-done | bytes 1310736 | tf_op jit(solution)/shard_map/all_gather | solution.py:89
  189.5 2.0 fusion.1
  191.5 12.8 %all_gather.19 = bf16[128,768]{0,1:T(8,128)(2,1)S(1)} all-gather(bf16[128,96]{0,1:T(8,128)(2,1)S(1)} %fusion.12), channel_id=1, replica_groups=mesh['head'=8,'ez'=16,'ey'=4] {'head'}, dimensions={1}, use_global_device_ids=true | all-gather | bytes 221184 | tf_op jit(solution)/shard_map/all_gather | solution.py:92
  205.4 13.5 %all-to-all-start.4 = ((bf16[64,2,640]{2,1,0:T(2,128)(2,1)}), bf16[64,2,640]{2,1,0:T(2,128)(2,1)S(1)}, u32[]{:S(2)}, u32[]{:S(2)}) async-start(bf16[64,2,640]{2,1,0:T(2,128)(2,1)} %reshape.58), calls=%async_computation.4 | async-start | bytes 327680 | tf_op jit(solution)/shard_map/all_to_all | solution.py:97
  219.1 18.2 %all-to-all-done.4 = bf16[64,2,640]{2,1,0:T(2,128)(2,1)S(1)} async-done(((bf16[64,2,640]{2,1,0:T(2,128)(2,1)}), bf16[64,2,640]{2,1,0:T(2,128)(2,1)S(1)}, u32[]{:S(2)}, u32[]{:S(2)}) %all-to-all-start.4) | async-done | bytes 163872 | tf_op jit(solution)/shard_map/all_to_all | solution.py:97
  237.4 0.8 convolution_add_fusion.1
  (45 shorter events, 7.3 us)
Async XLA Ops:
  6.5 182.9 %copy-start = (bf16[1,2,96,5120]{3,2,1,0:T(8,128)(2,1)S(1)}, bf16[1,2,96,5120]{3,2,1,0:T(8,128)(2,1)}, u32[]{:S(2)}) copy-start(bf16[1,2,96,5120]{3,2,1,0:T(8,128)(2,1)} %param.22) | copy-start | bytes 5898244
  6.5 3.6 %copy-start.1 = (bf16[8,128,512]{2,1,0:T(8,128)(2,1)S(1)}, bf16[8,128,512]{2,1,0:T(8,128)(2,1)}, u32[]{:S(2)}) copy-start(bf16[8,128,512]{2,1,0:T(8,128)(2,1)} %param.14) | copy-start | bytes 3145732
  6.5 49.3 %all-gather.8.cloned.1.call-start = ((), (), s32[]{:S(2)}) async-start(), calls=%async_computation.6 | async-start | bytes 3276800 | tf_op jit(solution)/shard_map/all_gather | solution.py:49
  11.6 65.2 %all-to-all-start = ((bf16[16,8,4096]{2,1,0:T(8,128)(2,1)}), bf16[16,8,4096]{2,1,0:T(8,128)(2,1)S(1)}, u32[]{:S(2)}, u32[]{:S(2)}) async-start(bf16[16,8,4096]{2,1,0:T(8,128)(2,1)} %broadcast_in_dim.33), calls=%async_computation | async-start | bytes 2097152 | tf_op jit(solution)/shard_map/all_to_all | solution.py:47
  26.8 82.4 %all-gather.10.cloned.1.call-start = ((), (), s32[]{:S(2)}) async-start(), calls=%async_computation.7 | async-start | bytes 1474560 | tf_op jit(solution)/shard_map/all_gather | solution.py:53
  76.8 3.3 %copy-start.3 = (s32[8,6]{1,0:T(8,128)S(1)}, s32[8,6]{1,0:T(8,128)}, u32[]{:S(2)}) copy-start(s32[8,6]{1,0:T(8,128)} %param.20) | copy-start | bytes 580
  110.7 27.4 %copy-start.2 = (bf16[8,5120]{1,0:T(8,128)(2,1)S(1)}, bf16[8,5120]{1,0:T(8,128)(2,1)}, u32[]{:S(2)}) copy-start(bf16[8,5120]{1,0:T(8,128)(2,1)} %param.18) | copy-start | bytes 245764
  111.8 26.1 %all-to-all-start.1 = ((bf16[16,8,320]{2,1,0:T(8,128)(2,1)}), bf16[16,8,320]{2,1,0:T(8,128)(2,1)S(1)}, u32[]{:S(2)}, u32[]{:S(2)}) async-start(bf16[16,8,320]{2,1,0:T(8,128)(2,1)} %bitcast.3), calls=%async_computation.1 | async-start | bytes 196608 | tf_op jit(solution)/shard_map/all_to_all | solution.py:54
  139.3 25.0 %all-to-all-start.2 = ((bf16[64,2,640]{2,1,0:T(2,128)(2,1)}), bf16[64,2,640]{2,1,0:T(2,128)(2,1)S(1)}, u32[]{:S(2)}, u32[]{:S(2)}) async-start(bf16[64,2,640]{2,1,0:T(2,128)(2,1)} %reshape.55), calls=%async_computation.2 | async-start | bytes 327680 | tf_op jit(solution)/shard_map/all_to_all | solution.py:82
  146.5 43.0 %all-gather.6.cloned.1.call-start = ((), (), s32[]{:S(2)}) async-start(), calls=%async_computation.5 | async-start | bytes 1474560 | tf_op jit(solution)/shard_map/all_gather | solution.py:89
  166.1 38.2 %all-to-all-start.3 = ((bf16[96,8,640]{2,0,1:T(8,128)(2,1)}), bf16[96,8,640]{2,0,1:T(8,128)(2,1)S(1)}, u32[]{:S(2)}, u32[]{:S(2)}) async-start(bf16[96,8,640]{2,0,1:T(8,128)(2,1)} %copy.26), calls=%async_computation.3 | async-start | bytes 1966080 | tf_op jit(solution)/shard_map/all_to_all | solution.py:87
  191.5 27.4 %copy-start.4 = (f32[8,6]{1,0:T(8,128)S(1)}, f32[8,6]{1,0:T(8,128)}, u32[]{:S(2)}) copy-start(f32[8,6]{1,0:T(8,128)} %param.21) | copy-start | bytes 580
  205.4 31.9 %all-to-all-start.4 = ((bf16[64,2,640]{2,1,0:T(2,128)(2,1)}), bf16[64,2,640]{2,1,0:T(2,128)(2,1)S(1)}, u32[]{:S(2)}, u32[]{:S(2)}) async-start(bf16[64,2,640]{2,1,0:T(2,128)(2,1)} %reshape.58), calls=%async_computation.4 | async-start | bytes 327680 | tf_op jit(solution)/shard_map/all_to_all | solution.py:97
Sparse Core Ops, SparseCore 0:
  9.5 46.3 all-gather.7
  80.2 28.9 all-gather.9
  165.2 24.2 all-gather.5
